TPU v7x, 256 devices: a whole 4x4x8 slice. The times are simulated.
256 devices in a mesh: pipe: 16 (over z, x_lo), ctx: 16 (over x_hi, y, core).
Axes of the slice: x: 4 (x_hi: 2, x_lo: 2; x = x_hi * 2 + x_lo), y: 4, z: 8, core: 2. Of those that a mesh axis runs over, the one named last changes fastest.
Arguments:
- forward_in: bfloat16 [16, 2, 512, 8192], P('pipe', None, 'ctx'), may hold values from -8 to 8
- backward_in: bfloat16 [16, 2, 512, 8192], P('pipe', None, 'ctx'), may hold values from -8 to 8
- grad_out: bfloat16 [16, 2, 512, 8192], P('pipe', None, 'ctx'), may hold values from -6 to 6
- cached_keys: bfloat16 [16, 2, 512, 8, 128], P('pipe', None, 'ctx'), may hold values from -21 to 21
- cached_values: bfloat16 [16, 2, 512, 8, 128], P('pipe', None, 'ctx'), may hold values from -6 to 6
- norm_gain: float32 [16, 2, 8192], P('pipe'), may hold values from 0.25 to 1.75
- key_weight: bfloat16 [16, 2, 8192, 1024], P('pipe', None, 'ctx'), may hold values from -0.0625 to 0.0625
- value_weight: bfloat16 [16, 2, 8192, 1024], P('pipe', None, 'ctx'), may hold values from -0.0625 to 0.0625
- segment_index: int32 [16, 2, 2], P('pipe'), may hold values from 0 to 1, as said below
Outputs:
- next_forward: bfloat16 [16, 2, 512, 8192], P('pipe', None, 'ctx')
- next_backward: bfloat16 [16, 2, 512, 8192], P('pipe', None, 'ctx')
Inputs may be any that keep to these rules, and one draw needn't show every extreme that they name: `segment_index`: the largest segment index, 1, occurs in every draw.
All inputs are finite; a program needn't handle non-finite values.
Results may differ from a plain program's by a relative error of at most 0.04.
Values may be sent and summed in bfloat16 or wider, within the bound.
No kernel may reach another device: no remote copies, remote signals or barrier semaphores. Data moves between devices by JAX's collectives and lax.ppermute only.
A program may use at most 128 MiB of HBM per device.

v0:
```python
import jax
import jax.numpy as jnp
from jax import lax
from jax.sharding import PartitionSpec as P

NEGATIVE = -1e30


def passed_along(array, axis, by):
    count = lax.axis_size(axis)
    return lax.ppermute(array, axis, [(i, (i + by) % count) for i in range(count)])


def normalize(in_rows, gain_row):
    as_float = in_rows.astype(jnp.float32)
    inverse = lax.rsqrt(jnp.mean(as_float * as_float, axis=-1, keepdims=True) + 1e-05)
    normed = as_float * inverse
    return (normed, inverse, (normed * gain_row).astype(jnp.bfloat16))


def probabilities(queries, key_list, position, cache_len):
    seg_len = queries.shape[0]
    factor = queries.shape[-1] ** (-0.5)
    scores = (
        jnp.einsum("tkgd,skd->kgts", queries, key_list, preferred_element_type=jnp.float32) * factor
    )
    column = lax.broadcasted_iota(jnp.int32, (seg_len, key_list.shape[0]), 1)
    row_ids = lax.broadcasted_iota(jnp.int32, (seg_len, key_list.shape[0]), 0)
    visible = jnp.where(
        column < cache_len, column < position * seg_len, column - cache_len <= row_ids
    )
    scores = jnp.where(visible, scores, NEGATIVE)
    row_max = jnp.max(scores, axis=-1, keepdims=True)
    lifted = jnp.exp(scores - row_max)
    return lifted / jnp.sum(lifted, axis=-1, keepdims=True)


def attend(queries, key_list, value_list, position, cache_len):
    prob_full = probabilities(queries, key_list, position, cache_len)
    prob_half = prob_full.astype(jnp.bfloat16)
    attended = jnp.einsum(
        "kgts,skd->tkgd", prob_half, value_list, preferred_element_type=jnp.float32
    )
    return (prob_full, prob_half, attended.astype(jnp.bfloat16))


def attend_back(queries, key_list, value_list, position, cache_len, grad_heads):
    prob_full, prob_half, attended = attend(queries, key_list, value_list, position, cache_len)
    grad_prob = jnp.einsum(
        "tkgd,skd->kgts", grad_heads, value_list, preferred_element_type=jnp.float32
    )
    row_delta = jnp.sum(grad_heads.astype(jnp.float32) * attended.astype(jnp.float32), axis=-1)
    row_delta = jnp.transpose(row_delta, (1, 2, 0))[..., None]
    factor = queries.shape[-1] ** (-0.5)
    grad_score = (prob_full * (grad_prob - row_delta) * factor).astype(jnp.bfloat16)
    grad_query = jnp.einsum(
        "kgts,skd->tkgd", grad_score, key_list, preferred_element_type=jnp.float32
    ).astype(jnp.bfloat16)
    grad_key = jnp.einsum(
        "kgts,tkgd->skd", grad_score[..., cache_len:], queries, preferred_element_type=jnp.float32
    ).astype(jnp.bfloat16)
    grad_value = jnp.einsum(
        "kgts,tkgd->skd", prob_half[..., cache_len:], grad_heads, preferred_element_type=jnp.float32
    ).astype(jnp.bfloat16)
    return (grad_query, grad_key, grad_value)


def input_grad(in_rows, gain_row, grad_acts, grad_rows):
    parts = normalize(in_rows, gain_row)
    normed = parts[0]
    inverse = parts[1]
    grad_normed = grad_acts.astype(jnp.float32) * gain_row
    grad_input = inverse * (
        grad_normed - normed * jnp.mean(grad_normed * normed, axis=-1, keepdims=True)
    )
    return (grad_rows.astype(jnp.float32) + grad_input).astype(jnp.bfloat16)


def on_device(
    forward_in,
    backward_in,
    grad_out,
    cached_keys,
    cached_values,
    norm_gain,
    key_weight,
    value_weight,
    segment_index,
):
    ctx_size = lax.axis_size("ctx")
    rank_id = lax.axis_index("ctx")
    stretch_count = forward_in.shape[1]
    local_rows = forward_in.shape[2]
    model_width = forward_in.shape[3]
    kv_count = cached_keys.shape[3]
    head_size = cached_keys.shape[4]
    seg_len = local_rows * ctx_size
    cache_local = cached_keys.shape[2]
    cache_len = cache_local * ctx_size
    head_count = model_width // head_size
    group_size = head_count // kv_count
    local_heads = head_count // ctx_size
    kv_local = max(1, local_heads // group_size)
    copies = max(1, group_size // local_heads)
    sub_heads = local_heads // kv_local
    first_kv = rank_id * local_heads // group_size
    every_key, every_value = (
        lax.all_gather(cached_keys[0], "ctx", axis=1, tiled=True),
        lax.all_gather(cached_values[0], "ctx", axis=1, tiled=True),
    )
    head_keys = lax.dynamic_slice_in_dim(every_key, first_kv, kv_local, 2)
    head_values = lax.dynamic_slice_in_dim(every_value, first_kv, kv_local, 2)

    def as_queries(block):
        return block.reshape(seg_len, kv_local, sub_heads, head_size)

    def own_heads(block):
        return lax.dynamic_slice_in_dim(
            block.reshape(seg_len, kv_count, head_size), first_kv, kv_local, 1
        )

    forward_outs = []
    backward_outs = []
    for stretch in range(stretch_count):
        gain_row = norm_gain[0, stretch]
        key_rows = key_weight[0, stretch]
        value_rows = value_weight[0, stretch]
        forward_rows = forward_in[0, stretch]
        backward_rows = backward_in[0, stretch]
        grad_rows = grad_out[0, stretch]
        forward_acts = normalize(forward_rows, gain_row)[2]
        backward_acts = normalize(backward_rows, gain_row)[2]
        sent = (
            lax.all_to_all(
                forward_acts.reshape(local_rows, ctx_size, -1),
                "ctx",
                split_axis=1,
                concat_axis=0,
                tiled=True,
            ),
            lax.all_to_all(
                backward_acts.reshape(local_rows, ctx_size, -1),
                "ctx",
                split_axis=1,
                concat_axis=0,
                tiled=True,
            ),
            lax.all_to_all(
                grad_rows.reshape(local_rows, ctx_size, -1),
                "ctx",
                split_axis=1,
                concat_axis=0,
                tiled=True,
            ),
        )
        forward_slice = sent[0].reshape(seg_len, -1)
        backward_slice = sent[1].reshape(seg_len, -1)
        partial_value = jnp.stack(
            [
                jnp.dot(forward_slice, key_rows, preferred_element_type=jnp.float32),
                jnp.dot(forward_slice, value_rows, preferred_element_type=jnp.float32),
                jnp.dot(backward_slice, key_rows, preferred_element_type=jnp.float32),
                jnp.dot(backward_slice, value_rows, preferred_element_type=jnp.float32),
            ]
        )
        new_kv = lax.psum(partial_value.astype(jnp.bfloat16), "ctx")
        forward_key_list = jnp.concatenate([head_keys[stretch], own_heads(new_kv[0])], axis=0)
        forward_value_list = jnp.concatenate([head_values[stretch], own_heads(new_kv[1])], axis=0)
        backward_key_list = jnp.concatenate([head_keys[stretch], own_heads(new_kv[2])], axis=0)
        backward_value_list = jnp.concatenate([head_values[stretch], own_heads(new_kv[3])], axis=0)
        attended = attend(
            as_queries(forward_slice),
            forward_key_list,
            forward_value_list,
            segment_index[0, stretch, 0],
            cache_len,
        )[2]
        grad_query, grad_key, grad_value = attend_back(
            as_queries(backward_slice),
            backward_key_list,
            backward_value_list,
            segment_index[0, stretch, 1],
            cache_len,
            as_queries(sent[2]),
        )
        run_sums = jnp.stack([grad_key.reshape(seg_len, -1), grad_value.reshape(seg_len, -1)])
        every_run = lax.all_gather(run_sums, "ctx", axis=2, tiled=True)
        kv_grads = jnp.sum(
            every_run.reshape(2, seg_len, kv_count, copies, head_size).astype(jnp.float32), axis=3
        ).astype(jnp.bfloat16)
        kv_grads = kv_grads.reshape(2, seg_len, kv_count * head_size)
        back_rows = jnp.einsum(
            "te,de->td", kv_grads[0], key_rows, preferred_element_type=jnp.float32
        )
        back_rows = back_rows + jnp.einsum(
            "te,de->td", kv_grads[1], value_rows, preferred_element_type=jnp.float32
        )
        grad_acts = (grad_query.reshape(seg_len, -1).astype(jnp.float32) + back_rows).astype(
            jnp.bfloat16
        )
        returned = (
            lax.all_to_all(
                attended.reshape(ctx_size, local_rows, -1),
                "ctx",
                split_axis=0,
                concat_axis=2,
                tiled=True,
            ),
            lax.all_to_all(
                grad_acts.reshape(ctx_size, local_rows, -1),
                "ctx",
                split_axis=0,
                concat_axis=2,
                tiled=True,
            ),
        )
        attn_rows = returned[0].reshape(local_rows, model_width)
        section_out = (forward_rows.astype(jnp.float32) + attn_rows.astype(jnp.float32)).astype(
            jnp.bfloat16
        )
        section_grad = input_grad(
            backward_rows, gain_row, returned[1].reshape(local_rows, model_width), grad_rows
        )
        forward_outs.append(section_out)
        backward_outs.append(section_grad)
    pipe_rank = lax.axis_index("pipe")
    arrived = passed_along(jnp.stack(forward_outs), "pipe", 1)
    next_forward = jnp.where(pipe_rank == 0, jnp.roll(arrived, 1, axis=0), arrived)
    came_back = passed_along(jnp.stack(backward_outs), "pipe", -1)
    next_backward = jnp.where(
        pipe_rank == lax.axis_size("pipe") - 1, jnp.roll(came_back, -1, axis=0), came_back
    )
    return (next_forward[None], next_backward[None])


def solution(mesh):
    in_specs = (
        P("pipe", None, "ctx", None),
        P("pipe", None, "ctx", None),
        P("pipe", None, "ctx", None),
        P("pipe", None, "ctx", None, None),
        P("pipe", None, "ctx", None, None),
        P("pipe", None, None),
        P("pipe", None, "ctx", None),
        P("pipe", None, "ctx", None),
        P("pipe", None, None),
    )
    out_specs = (P("pipe", None, "ctx", None), P("pipe", None, "ctx", None))
    return jax.shard_map(
        on_device, mesh=mesh, in_specs=in_specs, out_specs=out_specs, check_vma=False
    )
```

profile of v0, /device:TPU:1, one launch (start us, length us, event | category | flops | bytes accessed | tf_op | source)
XLA Modules:
  0.0 563.6 jit_solution(6010094165903002544)
XLA Ops:
  14.8 2.3 slice_convert_fusion.2
  22.4 8.4 %all-to-all-start.3 = ((bf16[32,16,512]{2,0,1:T(8,128)(2,1)}), bf16[32,16,512]{2,0,1:T(8,128)(2,1)}, u32[]{:S(2)}, u32[]{:S(2)}) async-start(bf16[32,16,512]{2,0,1:T(8,128)(2,1)} %copy.223), calls=%async_computation.3 | async-start | bytes 1048576 | tf_op jit(solution)/shard_map/all_to_all | solution.py:134
  33.6 8.7 %all-to-all-done.3 = bf16[32,16,512]{2,0,1:T(8,128)(2,1)} async-done(((bf16[32,16,512]{2,0,1:T(8,128)(2,1)}), bf16[32,16,512]{2,0,1:T(8,128)(2,1)}, u32[]{:S(2)}, u32[]{:S(2)}) %all-to-all-start.3) | async-done | bytes 524320 | tf_op jit(solution)/shard_map/all_to_all | solution.py:134
  42.3 4.5 all-to-all-start.1
  50.0 8.2 %all-to-all-done.1 = bf16[32,16,512]{2,0,1:T(8,128)(2,1)S(1)} async-done(((bf16[32,16,512]{2,0,1:T(8,128)(2,1)}), bf16[32,16,512]{2,0,1:T(8,128)(2,1)S(1)}, u32[]{:S(2)}, u32[]{:S(2)}) %all-to-all-start.1) | async-done | bytes 524320 | tf_op jit(solution)/shard_map/all_to_all | solution.py:141
  58.2 5.4 all-to-all-start
  63.5 2.9 fusion.43
  66.5 2.9 fusion.42
  69.4 3.1 fusion.45
  72.5 2.4 all-to-all-done
  74.9 5.1 all-to-all-start.4
  80.3 3.1 fusion.44
  83.4 2.9 fusion.41
  86.3 2.9 fusion.40
  89.2 2.3 all-to-all-done.4
  91.5 2.3 fusion.47
  95.9 3.8 pad_maximum_fusion
  104.2 5.1 all-to-all-start.6
  114.8 2.6 fusion.35
  117.4 8.1 %all-to-all-done.6 = bf16[32,16,512]{2,0,1:T(8,128)(2,1)} async-done(((bf16[32,16,512]{2,0,1:T(8,128)(2,1)}), bf16[32,16,512]{2,0,1:T(8,128)(2,1)}, u32[]{:S(2)}, u32[]{:S(2)}) %all-to-all-start.6) | async-done | bytes 524320 | tf_op jit(solution)/shard_map/all_to_all | solution.py:148
  125.5 6.1 %all-to-all-start.8 = ((bf16[32,16,512]{2,0,1:T(8,128)(2,1)}), bf16[32,16,512]{2,0,1:T(8,128)(2,1)}, u32[]{:S(2)}, u32[]{:S(2)}) async-start(bf16[32,16,512]{2,0,1:T(8,128)(2,1)} %copy.256), calls=%async_computation.8 | async-start | bytes 1048576 | tf_op jit(solution)/shard_map/all_to_all | solution.py:148
  131.6 2.3 copy_bitcast_fusion.1
  137.0 3.3 copy.240
  140.3 2.6 copy.242
  151.1 2.8 constant_dynamic-slice_fusion
  156.3 143.7 %all-reduce.3.cloned.1.call-done = (bf16[4,512,1024]{2,1,0:T(8,128)(2,1)}, bf16[4,512,1024]{2,1,0:T(8,128)(2,1)}) async-done(((bf16[4,512,1024]{2,1,0:T(8,128)(2,1)}, bf16[4,512,1024]{2,1,0:T(8,128)(2,1)}), (bf16[4,512,1024]{2,1,0:T(8,128)(2,1)}, bf16[4,512,1024]{2,1,0:T(8,128)(2,1)})) %all-reduce.3.cloned.1.call-update) | async-done | bytes 8388624 | tf_op jit(solution)/shard_map/psum | solution.py:166
  300.0 4.2 fusion.233
  304.2 2.7 copy.255
  306.9 2.3 copy.252
  310.2 4.4 fusion.232
  314.6 2.3 copy.289
  318.8 2.7 fusion.14
  323.1 3.6 fusion.9
  331.3 3.7 fusion.5
  337.8 2.3 copy_bitcast_fusion
  343.3 3.3 copy.261
  346.5 2.5 copy.263
  353.7 2.3 copy.226
  357.7 2.3 copy.225
  362.4 2.3 copy.287
  366.4 3.0 fusion.12
  371.2 4.3 fusion.6
  375.4 3.4 fusion.71
  383.0 7.9 %all-to-all-start.2 = ((bf16[16,32,512]{2,1,0:T(8,128)(2,1)}), bf16[16,32,512]{2,1,0:T(8,128)(2,1)}, u32[]{:S(2)}, u32[]{:S(2)}) async-start(bf16[16,32,512]{2,1,0:T(8,128)(2,1)} %reshape.802), calls=%async_computation.2 | async-start | bytes 1048576 | tf_op jit(solution)/shard_map/all_to_all | solution.py:202
  391.0 5.0 fusion.28
  396.8 5.7 %fusion.2 = bf16[1,4,512,1024]{2,3,1,0:T(8,128)(2,1)S(1)} fusion(f32[4,512]{1,0:T(4,128)S(1)} %bitcast.691, f32[4,512]{1,0:T(4,128)S(1)} %get-tuple-element.69, f32[4,512]{1,0:T(4,128)S(1)} %get-tuple-element.64, f32[1024,512,4]{1,0,2:T(8,128)} %copy-done, pred[512,1024]{0,1:T(8,128)(4,1)S(1)} %get-tuple-element.51, bf16[512,4,128]{2,1,0:T(4,128)(2,1)S(1)} %copy-done.25, ...), kind=kOutput, calls=%fused_computation.3 | convolution fusion | flops 554172416 | bytes 13918208 | tf_op jit(solution)/shard_map/tkgd,skd->kgts/dot_general | solution.py:49
  405.3 7.0 %fusion.68 = bf16[512,1,4,128]{0,3,2,1:T(8,128)(2,1)} fusion(f32[4,512]{1,0:T(4,128)} %get-tuple-element.67, f32[4,512]{1,0:T(4,128)} %copy-done.35, f32[1024,512,4]{1,0,2:T(8,128)} %copy-done.3, pred[512,1024]{0,1:T(8,128)(4,1)S(1)} %copy-done.15, bf16[512,1,128]{0,2,1:T(8,128)(2,1)} %bitcast.685, bf16[512,1,128]{0,2,1:T(8,128)(2,1)} %get-tuple-element.72), kind=kOutput, calls=%fused_computation.89 | convolution fusion | flops 548143104 | bytes 9715712 | tf_op jit(solution)/shard_map/kgts,skd->tkgd/dot_general | solution.py:41
  416.6 7.1 %all-to-all-start.5 = ((bf16[16,32,512]{2,1,0:T(8,128)(2,1)}), bf16[16,32,512]{2,1,0:T(8,128)(2,1)}, u32[]{:S(2)}, u32[]{:S(2)}) async-start(bf16[16,32,512]{2,1,0:T(8,128)(2,1)} %reshape.809), calls=%async_computation.5 | async-start | bytes 1048576 | tf_op jit(solution)/shard_map/all_to_all | solution.py:202
  426.0 9.2 %all-to-all-done.5 = bf16[16,32,512]{2,1,0:T(8,128)(2,1)} async-done(((bf16[16,32,512]{2,1,0:T(8,128)(2,1)}), bf16[16,32,512]{2,1,0:T(8,128)(2,1)}, u32[]{:S(2)}, u32[]{:S(2)}) %all-to-all-start.5) | async-done | bytes 524320 | tf_op jit(solution)/shard_map/all_to_all | solution.py:202
  439.5 4.0 fusion.98
  443.5 2.5 copy.249
  446.0 4.1 fusion.77
  450.1 2.5 copy.270
  452.6 19.7 %collective-permute-done = bf16[2,32,8192]{2,1,0:T(8,128)(2,1)S(1)} collective-permute-done((bf16[2,32,8192]{2,1,0:T(8,128)(2,1)}, bf16[2,32,8192]{2,1,0:T(8,128)(2,1)S(1)}, u32[]{:S(2)}, u32[]{:S(2)}) %collective-permute-start) | collective-permute-done | bytes 1048608 | tf_op jit(solution)/shard_map/ppermute | solution.py:11
  473.5 5.2 reduce_sum.153
  482.4 3.1 fusion.66
  485.5 8.3 %all-to-all-start.7 = ((bf16[16,32,512]{2,1,0:T(8,128)(2,1)}), bf16[16,32,512]{2,1,0:T(8,128)(2,1)}, u32[]{:S(2)}, u32[]{:S(2)}) async-start(bf16[16,32,512]{2,1,0:T(8,128)(2,1)} %bitcast.660), calls=%async_computation.7 | async-start | bytes 1048576 | tf_op jit(solution)/shard_map/all_to_all | solution.py:209
  493.8 5.0 reduce_sum.158
  502.6 3.2 fusion.67
  505.9 7.2 %all-to-all-start.9 = ((bf16[16,32,512]{2,1,0:T(8,128)(2,1)}), bf16[16,32,512]{2,1,0:T(8,128)(2,1)}, u32[]{:S(2)}, u32[]{:S(2)}) async-start(bf16[16,32,512]{2,1,0:T(8,128)(2,1)} %bitcast.661), calls=%async_computation.9 | async-start | bytes 1048576 | tf_op jit(solution)/shard_map/all_to_all | solution.py:209
  517.1 7.4 %all-to-all-done.9 = bf16[16,32,512]{2,1,0:T(8,128)(2,1)} async-done(((bf16[16,32,512]{2,1,0:T(8,128)(2,1)}), bf16[16,32,512]{2,1,0:T(8,128)(2,1)}, u32[]{:S(2)}, u32[]{:S(2)}) %all-to-all-start.9) | async-done | bytes 524320 | tf_op jit(solution)/shard_map/all_to_all | solution.py:209
  529.9 4.3 collective-permute-start.1
  534.2 2.3 fusion.142
  536.5 19.0 %collective-permute-done.1 = bf16[2,32,8192]{2,1,0:T(8,128)(2,1)S(1)} collective-permute-done((bf16[2,32,8192]{2,1,0:T(8,128)(2,1)S(1)}, bf16[2,32,8192]{2,1,0:T(8,128)(2,1)S(1)}, u32[]{:S(2)}, u32[]{:S(2)}) %collective-permute-start.1) | collective-permute-done | bytes 1048608 | tf_op jit(solution)/shard_map/ppermute | solution.py:11
  (199 shorter events, 107.0 us)
Async XLA Ops:
  7.2 10.0 %copy-start.34 = (f32[1,2,8192]{2,1,0:T(2,128)S(1)}, f32[1,2,8192]{2,1,0:T(2,128)}, u32[]{:S(2)}) copy-start(f32[1,2,8192]{2,1,0:T(2,128)} %param.14) | copy-start | bytes 196612
  7.2 143.9 %all-gather.11.cloned.1.call-start = ((), (), s32[]{:S(2)}) async-start(), calls=%async_computation.12 | async-start | bytes 2228224 | tf_op jit(solution)/shard_map/all_gather | solution.py:109
  8.8 145.8 %all-gather.13.cloned.1.call-start = ((), (), s32[]{:S(2)}) async-start(), calls=%async_computation.13 | async-start | bytes 2228224 | tf_op jit(solution)/shard_map/all_gather | solution.py:108
  17.2 15.3 %copy-start.36 = (f32[32]{0:T(128)}, f32[32]{0:T(128)S(1)}, u32[]{:S(2)}) copy-start(f32[32]{0:T(128)S(1)} %add_rsqrt_fusion) | copy-start | bytes 388
  17.9 14.6 %copy-start.27 = (f32[16,512]{1,0:T(8,128)}, f32[16,512]{1,0:T(8,128)S(1)}, u32[]{:S(2)}) copy-start(f32[16,512]{1,0:T(8,128)S(1)} %mul.356) | copy-start | bytes 98308
  22.4 19.8 %all-to-all-start.3 = ((bf16[32,16,512]{2,0,1:T(8,128)(2,1)}), bf16[32,16,512]{2,0,1:T(8,128)(2,1)}, u32[]{:S(2)}, u32[]{:S(2)}) async-start(bf16[32,16,512]{2,0,1:T(8,128)(2,1)} %copy.223), calls=%async_computation.3 | async-start | bytes 1048576 | tf_op jit(solution)/shard_map/all_to_all | solution.py:134
  30.9 38.5 %copy-start.29 = (f32[16,512]{1,0:T(8,128)}, f32[16,512]{1,0:T(8,128)S(1)}, u32[]{:S(2)}) copy-start(f32[16,512]{1,0:T(8,128)S(1)} %mul.341) | copy-start | bytes 98308
  32.2 40.4 %copy-start.38 = (f32[32]{0:T(128)}, f32[32]{0:T(128)S(1)}, u32[]{:S(2)}) copy-start(f32[32]{0:T(128)S(1)} %add_rsqrt_fusion.2) | copy-start | bytes 388
  42.3 15.9 %all-to-all-start.1 = ((bf16[32,16,512]{2,0,1:T(8,128)(2,1)}), bf16[32,16,512]{2,0,1:T(8,128)(2,1)S(1)}, u32[]{:S(2)}, u32[]{:S(2)}) async-start(bf16[32,16,512]{2,0,1:T(8,128)(2,1)} %copy.215), calls=%async_computation.1 | async-start | bytes 1048576 | tf_op jit(solution)/shard_map/all_to_all | solution.py:141
  58.2 28.1 %copy-start.17 = (bf16[32,16,512]{2,0,1:T(8,128)(2,1)}, bf16[32,16,512]{2,0,1:T(8,128)(2,1)S(1)}, u32[]{:S(2)}) copy-start(bf16[32,16,512]{2,0,1:T(8,128)(2,1)S(1)} %all-to-all-done.1) | copy-start | bytes 1572868
  58.2 16.7 %all-to-all-start = ((bf16[32,16,512]{2,0,1:T(8,128)(2,1)}), bf16[32,16,512]{2,0,1:T(8,128)(2,1)S(1)}, u32[]{:S(2)}, u32[]{:S(2)}) async-start(bf16[32,16,512]{2,0,1:T(8,128)(2,1)} %copy.214), calls=%async_computation | async-start | bytes 1048576 | tf_op jit(solution)/shard_map/all_to_all | solution.py:134
  74.9 21.0 %copy-start.13 = (bf16[32,16,512]{2,0,1:T(8,128)(2,1)}, bf16[32,16,512]{2,0,1:T(8,128)(2,1)S(1)}, u32[]{:S(2)}) copy-start(bf16[32,16,512]{2,0,1:T(8,128)(2,1)S(1)} %all-to-all-done) | copy-start | bytes 1572868
  74.9 16.6 %all-to-all-start.4 = ((bf16[32,16,512]{2,0,1:T(8,128)(2,1)}), bf16[32,16,512]{2,0,1:T(8,128)(2,1)}, u32[]{:S(2)}, u32[]{:S(2)}) async-start(bf16[32,16,512]{2,0,1:T(8,128)(2,1)} %copy.224), calls=%async_computation.4 | async-start | bytes 1048576 | tf_op jit(solution)/shard_map/all_to_all | solution.py:141
  80.1 219.9 %all-reduce.3.cloned.1.call-start = ((), (), s32[]{:S(2)}) async-start(), calls=%async_computation.14 | async-start | bytes 16777216 | tf_op jit(solution)/shard_map/psum | solution.py:166
  91.5 8.2 %copy-start.18 = (bf16[1,512,1024]{2,1,0:T(8,128)(2,1)S(1)}, bf16[1,512,1024]{2,1,0:T(8,128)(2,1)}, u32[]{:S(2)}) copy-start(bf16[1,512,1024]{2,1,0:T(8,128)(2,1)} %fusion.45) | copy-start | bytes 3145732
  91.5 8.2 %copy-start.19 = (bf16[1,512,1024]{2,1,0:T(8,128)(2,1)S(1)}, bf16[1,512,1024]{2,1,0:T(8,128)(2,1)}, u32[]{:S(2)}) copy-start(bf16[1,512,1024]{2,1,0:T(8,128)(2,1)} %fusion.44) | copy-start | bytes 3145732
  99.8 2.3 copy-start.4
  102.1 7.3 %copy-start.40 = (s32[1,2,2]{2,1,0:T(2,128)S(1)}, s32[1,2,2]{2,1,0:T(2,128)}, u32[]{:S(2)}) copy-start(s32[1,2,2]{2,1,0:T(2,128)} %param.17) | copy-start | bytes 52
  104.2 21.3 %all-to-all-start.6 = ((bf16[32,16,512]{2,0,1:T(8,128)(2,1)}), bf16[32,16,512]{2,0,1:T(8,128)(2,1)}, u32[]{:S(2)}, u32[]{:S(2)}) async-start(bf16[32,16,512]{2,0,1:T(8,128)(2,1)} %copy.235), calls=%async_computation.6 | async-start | bytes 1048576 | tf_op jit(solution)/shard_map/all_to_all | solution.py:148
  125.5 212.4 %all-to-all-start.8 = ((bf16[32,16,512]{2,0,1:T(8,128)(2,1)}), bf16[32,16,512]{2,0,1:T(8,128)(2,1)}, u32[]{:S(2)}, u32[]{:S(2)}) async-start(bf16[32,16,512]{2,0,1:T(8,128)(2,1)} %copy.256), calls=%async_computation.8 | async-start | bytes 1048576 | tf_op jit(solution)/shard_map/all_to_all | solution.py:148
  131.5 342.0 %all-gather.7.cloned.1.call-start = ((), (), s32[]{:S(2)}) async-start(), calls=%async_computation.10 | async-start | bytes 4456448 | tf_op jit(solution)/shard_map/all_gather | solution.py:187
  316.9 4.6 copy-start.10
  323.1 3.7 copy-start
  326.7 3.8 copy-start.8
  326.7 3.7 copy-start.20
  326.7 4.5 copy-start.24
  331.3 3.8 copy-start.12
  335.1 2.0 copy-start.5
  335.1 14.0 %copy-start.14 = (bf16[32,16,512]{2,0,1:T(8,128)(2,1)S(1)}, bf16[32,16,512]{2,0,1:T(8,128)(2,1)}, u32[]{:S(2)}) copy-start(bf16[32,16,512]{2,0,1:T(8,128)(2,1)} %copy-done.13) | copy-start | bytes 1572868
  357.7 11.8 %copy-start.15 = (pred[512,1024]{0,1:T(8,128)(4,1)S(1)}, pred[512,1024]{0,1:T(8,128)(4,1)}, u32[]{:S(2)}) copy-start(pred[512,1024]{0,1:T(8,128)(4,1)} %get-tuple-element.52) | copy-start | bytes 1572868
  364.7 4.7 copy-start.26
  364.7 4.7 copy-start.33
  366.4 4.7 copy-start.16
  371.1 4.3 copy-start.3
  371.1 4.3 copy-start.35
  371.2 4.3 copy-start.21
  383.0 33.6 %all-to-all-start.2 = ((bf16[16,32,512]{2,1,0:T(8,128)(2,1)}), bf16[16,32,512]{2,1,0:T(8,128)(2,1)}, u32[]{:S(2)}, u32[]{:S(2)}) async-start(bf16[16,32,512]{2,1,0:T(8,128)(2,1)} %reshape.802), calls=%async_computation.2 | async-start | bytes 1048576 | tf_op jit(solution)/shard_map/all_to_all | solution.py:202
  390.9 102.9 %all-gather.9.cloned.1.call-start = ((), (), s32[]{:S(2)}) async-start(), calls=%async_computation.11 | async-start | bytes 4456448 | tf_op jit(solution)/shard_map/all_gather | solution.py:187
  390.9 5.0 copy-start.9
  390.9 5.0 copy-start.22
  391.0 5.0 copy-start.23
  391.0 5.8 %copy-start.25 = (bf16[512,4,128]{2,1,0:T(4,128)(2,1)S(1)}, bf16[512,4,128]{2,1,0:T(4,128)(2,1)}, u32[]{:S(2)}) copy-start(bf16[512,4,128]{2,1,0:T(4,128)(2,1)} %reshape.823) | copy-start | bytes 1572868
  396.8 5.7 %copy-start.11 = (bf16[512,4,128]{0,2,1:T(8,128)(2,1)S(1)}, bf16[512,4,128]{0,2,1:T(8,128)(2,1)}, u32[]{:S(2)}) copy-start(bf16[512,4,128]{0,2,1:T(8,128)(2,1)} %copy.266) | copy-start | bytes 1572868
  402.5 2.0 copy-start.6
  412.3 24.0 %copy-start.2 = (bf16[1,2,32,8192]{3,2,1,0:T(8,128)(2,1)S(1)}, bf16[1,2,32,8192]{3,2,1,0:T(8,128)(2,1)}, u32[]{:S(2)}) copy-start(bf16[1,2,32,8192]{3,2,1,0:T(8,128)(2,1)} %param.9) | copy-start | bytes 3145732
  416.6 18.5 %all-to-all-start.5 = ((bf16[16,32,512]{2,1,0:T(8,128)(2,1)}), bf16[16,32,512]{2,1,0:T(8,128)(2,1)}, u32[]{:S(2)}, u32[]{:S(2)}) async-start(bf16[16,32,512]{2,1,0:T(8,128)(2,1)} %reshape.809), calls=%async_computation.5 | async-start | bytes 1048576 | tf_op jit(solution)/shard_map/all_to_all | solution.py:202
  438.9 33.4 %collective-permute-start = (bf16[2,32,8192]{2,1,0:T(8,128)(2,1)}, bf16[2,32,8192]{2,1,0:T(8,128)(2,1)S(1)}, u32[]{:S(2)}, u32[]{:S(2)}) collective-permute-start(bf16[2,32,8192]{2,1,0:T(8,128)(2,1)} %pad_maximum_fusion.2), channel_id=1, source_target_pairs={{0,16},{16,32},{32,48},{48,64},{64,80},{80,96},{96,112},{112,128},... | collective-permute-start | bytes 3145736 | tf_op jit(solution)/shard_map/ppermute | solution.py:11
  472.3 13.2 %copy-start.7 = (bf16[2,32,8192]{2,1,0:T(8,128)(2,1)}, bf16[2,32,8192]{2,1,0:T(8,128)(2,1)S(1)}, u32[]{:S(2)}) copy-start(bf16[2,32,8192]{2,1,0:T(8,128)(2,1)S(1)} %collective-permute-done) | copy-start | bytes 3145732
  485.5 20.3 %all-to-all-start.7 = ((bf16[16,32,512]{2,1,0:T(8,128)(2,1)}), bf16[16,32,512]{2,1,0:T(8,128)(2,1)}, u32[]{:S(2)}, u32[]{:S(2)}) async-start(bf16[16,32,512]{2,1,0:T(8,128)(2,1)} %bitcast.660), calls=%async_computation.7 | async-start | bytes 1048576 | tf_op jit(solution)/shard_map/all_to_all | solution.py:209
  498.8 16.5 %copy-start.30 = (f32[16,512]{1,0:T(8,128)S(1)}, f32[16,512]{1,0:T(8,128)}, u32[]{:S(2)}) copy-start(f32[16,512]{1,0:T(8,128)} %copy-done.29) | copy-start | bytes 98308
  498.8 16.5 %copy-start.39 = (f32[32]{0:T(128)S(1)}, f32[32]{0:T(128)}, u32[]{:S(2)}) copy-start(f32[32]{0:T(128)} %copy-done.38) | copy-start | bytes 388
  498.8 25.7 %copy-start.28 = (f32[16,512]{1,0:T(8,128)S(1)}, f32[16,512]{1,0:T(8,128)}, u32[]{:S(2)}) copy-start(f32[16,512]{1,0:T(8,128)} %copy-done.27) | copy-start | bytes 98308
  498.8 25.7 %copy-start.37 = (f32[32]{0:T(128)S(1)}, f32[32]{0:T(128)}, u32[]{:S(2)}) copy-start(f32[32]{0:T(128)} %copy-done.36) | copy-start | bytes 388
  502.6 25.0 %copy-start.1 = (bf16[1,2,32,8192]{3,2,1,0:T(8,128)(2,1)S(1)}, bf16[1,2,32,8192]{3,2,1,0:T(8,128)(2,1)}, u32[]{:S(2)}) copy-start(bf16[1,2,32,8192]{3,2,1,0:T(8,128)(2,1)} %param.10) | copy-start | bytes 3145732
  502.6 25.0 %copy-start.31 = (f32[1,1,8192]{2,1,0:T(1,128)S(1)}, f32[1,1,8192]{2,1,0:T(1,128)}, u32[]{:S(2)}) copy-start(f32[1,1,8192]{2,1,0:T(1,128)} %get-tuple-element.44) | copy-start | bytes 98308
  502.6 25.0 %copy-start.32 = (f32[1,1,8192]{2,1,0:T(1,128)S(1)}, f32[1,1,8192]{2,1,0:T(1,128)}, u32[]{:S(2)}) copy-start(f32[1,1,8192]{2,1,0:T(1,128)} %get-tuple-element.45) | copy-start | bytes 98308
  505.9 18.6 %all-to-all-start.9 = ((bf16[16,32,512]{2,1,0:T(8,128)(2,1)}), bf16[16,32,512]{2,1,0:T(8,128)(2,1)}, u32[]{:S(2)}, u32[]{:S(2)}) async-start(bf16[16,32,512]{2,1,0:T(8,128)(2,1)} %bitcast.661), calls=%async_computation.9 | async-start | bytes 1048576 | tf_op jit(solution)/shard_map/all_to_all | solution.py:209
  529.9 25.6 %collective-permute-start.1 = (bf16[2,32,8192]{2,1,0:T(8,128)(2,1)S(1)}, bf16[2,32,8192]{2,1,0:T(8,128)(2,1)S(1)}, u32[]{:S(2)}, u32[]{:S(2)}) collective-permute-start(bf16[2,32,8192]{2,1,0:T(8,128)(2,1)S(1)} %pad_maximum_fusion.3), channel_id=1, source_target_pairs={{0,240},{16,0},{32,16},{48,32},{64,48},{80,64},{96,80},{112,96},{1... | collective-permute-start | bytes 3145736 | tf_op jit(solution)/shard_map/ppermute | solution.py:11
Sparse Core Ops, SparseCore 0:
  10.8 60.4 all-gather.10
  73.8 58.7 all-gather.12
  135.3 164.6 all-reduce.2
  338.0 67.3 all-gather.6
  408.0 74.6 all-gather.8
where the time goes:
time: 573 us; the launch traced here: 564 us
  waiting for transfers between devices  229 us (40%)
  local copies, waits for them, and re-layouts  108 us (19%)
  matrix products  74.3 us (13%)
  starting transfers between devices  70.5 us (12%)
  other arithmetic  64.4 us (11%)
  between operations  17.5 us (3%)
    psum x1, waiting for transfers between devices, on_device(): new_kv = lax.psum(partial_value.astype(jnp.bfloat16), 'ctx')  144 us
    ppermute x2, waiting for transfers between devices, passed_along(): lax.ppermute(array, axis, [(i, (i + by) % count) for i in range(count)])  38.7 us
    unnamed x98, local copies, waits for them, and re-layouts  16.2 us
    all_to_all x2, starting transfers between devices, on_device(): lax.all_to_all(grad_acts.reshape(ctx_size, local_rows, -1), 'ctx', split_...  15.5 us
    another operation x8, local copies, waits for them, and re-layouts  15.1 us
    all_to_all x2, starting transfers between devices, on_device(): lax.all_to_all(attended.reshape(ctx_size, local_rows, -1), 'ctx', split_a...  15 us
    all_to_all x2, starting transfers between devices, on_device(): lax.all_to_all(forward_acts.reshape(local_rows, ctx_size, -1), 'ctx', spl...  13.8 us
    dot_general x4, matrix products, attend(): jnp.einsum('kgts,skd->tkgd', prob_half, value_list, preferred_element_typ...  12 us
  transfers between devices with their start and end apart: 17, of which 10 were waited for; matrix products, arithmetic and copies ran while one was open for 42% of the time, Pallas kernels for 0%

commit v1 on v0

v1 whole, which is shorter than its diff:
```python
import jax
import jax.numpy as jnp
from jax import lax
from jax.sharding import PartitionSpec as P

NEGATIVE = -1e30


def passed_along(array, axis, by):
    count = lax.axis_size(axis)
    return lax.ppermute(array, axis, [(i, (i + by) % count) for i in range(count)])


def swapped_pairs(array, axis):
    count = lax.axis_size(axis)
    return lax.ppermute(array, axis, [(i, i ^ 1) for i in range(count)])


def normalize(in_rows, gain_row):
    as_float = in_rows.astype(jnp.float32)
    inverse = lax.rsqrt(jnp.mean(as_float * as_float, axis=-1, keepdims=True) + 1e-05)
    normed = as_float * inverse
    return (normed, inverse, (normed * gain_row).astype(jnp.bfloat16))


def probabilities(queries, key_list, position, cache_len):
    seg_len = queries.shape[0]
    factor = queries.shape[-1] ** (-0.5)
    scores = (
        jnp.einsum("tgd,sd->gts", queries, key_list, preferred_element_type=jnp.float32) * factor
    )
    column = lax.broadcasted_iota(jnp.int32, (seg_len, key_list.shape[0]), 1)
    row_ids = lax.broadcasted_iota(jnp.int32, (seg_len, key_list.shape[0]), 0)
    visible = jnp.where(
        column < cache_len, column < position * seg_len, column - cache_len <= row_ids
    )
    scores = jnp.where(visible, scores, NEGATIVE)
    row_max = jnp.max(scores, axis=-1, keepdims=True)
    lifted = jnp.exp(scores - row_max)
    return lifted / jnp.sum(lifted, axis=-1, keepdims=True)


def attend(queries, key_list, value_list, position, cache_len):
    prob_full = probabilities(queries, key_list, position, cache_len)
    prob_half = prob_full.astype(jnp.bfloat16)
    attended = jnp.einsum(
        "gts,sd->tgd", prob_half, value_list, preferred_element_type=jnp.float32
    )
    return (prob_full, prob_half, attended.astype(jnp.bfloat16))


def attend_back(queries, key_list, value_list, position, cache_len, grad_heads):
    prob_full, prob_half, attended = attend(queries, key_list, value_list, position, cache_len)
    grad_prob = jnp.einsum(
        "tgd,sd->gts", grad_heads, value_list, preferred_element_type=jnp.float32
    )
    row_delta = jnp.sum(grad_heads.astype(jnp.float32) * attended.astype(jnp.float32), axis=-1)
    row_delta = jnp.transpose(row_delta, (1, 0))[..., None]
    factor = queries.shape[-1] ** (-0.5)
    grad_score = (prob_full * (grad_prob - row_delta) * factor).astype(jnp.bfloat16)
    grad_query = jnp.einsum(
        "gts,sd->tgd", grad_score, key_list, preferred_element_type=jnp.float32
    ).astype(jnp.bfloat16)
    grad_key = jnp.einsum(
        "gts,tgd->sd", grad_score[..., cache_len:], queries, preferred_element_type=jnp.float32
    )
    grad_value = jnp.einsum(
        "gts,tgd->sd", prob_half[..., cache_len:], grad_heads, preferred_element_type=jnp.float32
    )
    return (grad_query, grad_key.astype(jnp.bfloat16), grad_value.astype(jnp.bfloat16))


def input_grad(in_rows, gain_row, grad_acts, grad_rows):
    parts = normalize(in_rows, gain_row)
    normed = parts[0]
    inverse = parts[1]
    grad_normed = grad_acts.astype(jnp.float32) * gain_row
    grad_input = inverse * (
        grad_normed - normed * jnp.mean(grad_normed * normed, axis=-1, keepdims=True)
    )
    return (grad_rows.astype(jnp.float32) + grad_input).astype(jnp.bfloat16)


def on_device(
    forward_in,
    backward_in,
    grad_out,
    cached_keys,
    cached_values,
    norm_gain,
    key_weight,
    value_weight,
    segment_index,
):
    ctx_size = lax.axis_size("ctx")
    rank_id = lax.axis_index("ctx")
    stretch_count = forward_in.shape[1]
    local_rows = forward_in.shape[2]
    model_width = forward_in.shape[3]
    kv_count = cached_keys.shape[3]
    head_size = cached_keys.shape[4]
    seg_len = local_rows * ctx_size
    cache_local = cached_keys.shape[2]
    cache_len = cache_local * ctx_size
    head_count = model_width // head_size
    group_size = head_count // kv_count
    local_heads = head_count // ctx_size
    local_width = model_width // ctx_size
    kv_width = kv_count * head_size
    piece = kv_width // ctx_size
    copies = ctx_size // kv_count
    is_even = rank_id % 2 == 0

    def per_owner(cache):
        picked = jnp.repeat(cache[0], copies, axis=2)
        return jnp.transpose(picked, (1, 2, 0, 3)).reshape(cache_local, ctx_size, -1)

    cache_rows = jnp.concatenate([per_owner(cached_keys), per_owner(cached_values)], axis=-1)

    forward_outs = []
    backward_outs = []
    for stretch in range(stretch_count):
        gain_row = norm_gain[0, stretch]
        key_rows = key_weight[0, stretch]
        value_rows = value_weight[0, stretch]
        forward_rows = forward_in[0, stretch]
        backward_rows = backward_in[0, stretch]
        grad_rows = grad_out[0, stretch]
        forward_acts = normalize(forward_rows, gain_row)[2]
        backward_acts = normalize(backward_rows, gain_row)[2]
        outgoing = [
            forward_acts.reshape(local_rows, ctx_size, local_width),
            backward_acts.reshape(local_rows, ctx_size, local_width),
            grad_rows.reshape(local_rows, ctx_size, local_width),
        ]
        if stretch == 0:
            outgoing.append(cache_rows)
        sent = lax.all_to_all(
            jnp.stack(outgoing), "ctx", split_axis=2, concat_axis=1, tiled=True
        )
        if stretch == 0:
            cache_heads = sent[3].reshape(cache_len, 2, stretch_count, head_size)
        forward_slice = sent[0].reshape(seg_len, local_width)
        backward_slice = sent[1].reshape(seg_len, local_width)
        grad_slice = sent[2].reshape(seg_len, local_width)
        both_slices = jnp.stack([forward_slice, backward_slice])
        key_pieces = key_rows.reshape(local_width, ctx_size, piece)
        value_pieces = value_rows.reshape(local_width, ctx_size, piece)
        partial_value = jnp.stack(
            [
                jnp.einsum("btf,fce->bcte", both_slices, key_pieces, preferred_element_type=jnp.float32),
                jnp.einsum("btf,fce->bcte", both_slices, value_pieces, preferred_element_type=jnp.float32),
            ],
            axis=1,
        ).astype(jnp.bfloat16)
        mine = lax.psum_scatter(
            partial_value.reshape(4, ctx_size, -1), "ctx", scatter_dimension=1, tiled=True
        ).reshape(2, 2, seg_len, piece)
        theirs = swapped_pairs(mine, "ctx")
        new_kv = jnp.where(
            is_even,
            jnp.concatenate([mine, theirs], axis=-1),
            jnp.concatenate([theirs, mine], axis=-1),
        )
        cached_k = cache_heads[:, 0, stretch]
        cached_v = cache_heads[:, 1, stretch]
        forward_key_list = jnp.concatenate([cached_k, new_kv[0, 0]], axis=0)
        forward_value_list = jnp.concatenate([cached_v, new_kv[0, 1]], axis=0)
        backward_key_list = jnp.concatenate([cached_k, new_kv[1, 0]], axis=0)
        backward_value_list = jnp.concatenate([cached_v, new_kv[1, 1]], axis=0)
        attended = attend(
            forward_slice.reshape(seg_len, local_heads, head_size),
            forward_key_list,
            forward_value_list,
            segment_index[0, stretch, 0],
            cache_len,
        )[2]
        grad_query, grad_key, grad_value = attend_back(
            backward_slice.reshape(seg_len, local_heads, head_size),
            backward_key_list,
            backward_value_list,
            segment_index[0, stretch, 1],
            cache_len,
            grad_slice.reshape(seg_len, local_heads, head_size),
        )
        run_sums = jnp.stack([grad_key, grad_value])
        other_run = swapped_pairs(run_sums, "ctx")
        head_grads = (run_sums.astype(jnp.float32) + other_run.astype(jnp.float32)).astype(
            jnp.bfloat16
        )
        half_rows = seg_len // 2
        my_half = lax.dynamic_slice_in_dim(head_grads, (rank_id % 2) * half_rows, half_rows, 1)
        every_half = lax.all_gather(my_half, "ctx", axis=0, tiled=False)
        every_half = every_half.reshape(kv_count, 2, 2, half_rows, head_size)
        key_rows_heads = key_rows.reshape(local_width, kv_count, head_size)
        value_rows_heads = value_rows.reshape(local_width, kv_count, head_size)
        back_rows = jnp.einsum(
            "jhtd,fjd->htf", every_half[:, :, 0], key_rows_heads, preferred_element_type=jnp.float32
        )
        back_rows = back_rows + jnp.einsum(
            "jhtd,fjd->htf",
            every_half[:, :, 1],
            value_rows_heads,
            preferred_element_type=jnp.float32,
        )
        grad_acts = (
            grad_query.reshape(seg_len, -1).astype(jnp.float32) + back_rows.reshape(seg_len, -1)
        ).astype(jnp.bfloat16)
        returned = lax.all_to_all(
            jnp.stack([attended.reshape(ctx_size, local_rows, -1), grad_acts.reshape(ctx_size, local_rows, -1)]),
            "ctx",
            split_axis=1,
            concat_axis=3,
            tiled=True,
        )
        attn_rows = returned[0].reshape(local_rows, model_width)
        section_out = (forward_rows.astype(jnp.float32) + attn_rows.astype(jnp.float32)).astype(
            jnp.bfloat16
        )
        section_grad = input_grad(
            backward_rows, gain_row, returned[1].reshape(local_rows, model_width), grad_rows
        )
        forward_outs.append(passed_along(section_out, "pipe", 1))
        backward_outs.append(passed_along(section_grad, "pipe", -1))
    pipe_rank = lax.axis_index("pipe")
    arrived = jnp.stack(forward_outs)
    next_forward = jnp.where(pipe_rank == 0, jnp.roll(arrived, 1, axis=0), arrived)
    came_back = jnp.stack(backward_outs)
    next_backward = jnp.where(
        pipe_rank == lax.axis_size("pipe") - 1, jnp.roll(came_back, -1, axis=0), came_back
    )
    return (next_forward[None], next_backward[None])


def solution(mesh):
    in_specs = (
        P("pipe", None, "ctx", None),
        P("pipe", None, "ctx", None),
        P("pipe", None, "ctx", None),
        P("pipe", None, "ctx", None, None),
        P("pipe", None, "ctx", None, None),
        P("pipe", None, None),
        P("pipe", None, "ctx", None),
        P("pipe", None, "ctx", None),
        P("pipe", None, None),
    )
    out_specs = (P("pipe", None, "ctx", None), P("pipe", None, "ctx", None))
    return jax.shard_map(
        on_device, mesh=mesh, in_specs=in_specs, out_specs=out_specs, check_vma=False
    )
```

time: 573 us -> 548 us (0.956)
  starting transfers between devices: 70.5 us -> 33.5 us
  local copies, waits for them, and re-layouts: 108 us -> 142 us
  other arithmetic: 64.4 us -> 41 us
  waiting for transfers between devices: 229 us -> 236 us
  matrix products: 74.3 us -> 67.5 us
    psum x1 -> x0, waiting for transfers between devices: 144 us -> none  [on_device(): new_kv = lax.psum(partial_value.astype(jnp.bfloat16), 'ctx')]
    unnamed x5 -> x4, waiting for transfers between devices: 0.08 us -> 141 us
    all_to_all x10 -> x4, starting transfers between devices: 65.1 us -> 24.1 us  [the longest x2 13.7 us: on_device(): lax.all_to_all(jnp.stack(outgoing), 'ctx', split_axis=2, concat_axis=1, t...]
    dot_general x28 -> x20, matrix products: 74.3 us -> 36.8 us  [the longest x4 11.7 us: attend(): jnp.einsum('gts,sd->tgd', prob_half, value_list, preferred_element_type=j...]
    sub x0 -> x4, matrix products: none -> 30.8 us  [probabilities(): lifted = jnp.exp(scores - row_max)]
    convert_element_type x14 -> x8, local copies, waits for them, and re-layouts: 24.4 us -> 55 us  [the longest x4 44.5 us: on_device(): partial_value = jnp.stack([jnp.einsum('btf,fce->bcte', both_slices, key_p...]
    all_gather x4 -> x2, waiting for transfers between devices: 0.02 us -> 26.7 us  [on_device(): every_half = lax.all_gather(my_half, 'ctx', axis=0, tiled=False)]
    all_to_all x10 -> x4, waiting for transfers between devices: 46.2 us -> 25.5 us  [the longest x2 13.9 us: on_device(): lax.all_to_all(jnp.stack(outgoing), 'ctx', split_axis=2, concat_axis=1, t...]
  transfers between devices with their start and end apart: 17 -> 15, of which waited for: 10 -> 7; matrix products, arithmetic and copies ran while one was open for 42% -> 36% of each run, Pallas kernels for 0% -> 0%
where the time goes in v1:
time: 548 us; the launch traced here: 538 us
  waiting for transfers between devices  236 us (43%)
  local copies, waits for them, and re-layouts  142 us (26%)
  matrix products  67.5 us (12%)
  other arithmetic  41 us (7%)
  starting transfers between devices  33.5 us (6%)
  between operations  17.7 us (3%)
    unnamed x4, waiting for transfers between devices  141 us
    convert_element_type x4, local copies, waits for them, and re-layouts, on_device(): partial_value = jnp.stack([jnp.einsum('btf,fce->bcte', both_slices, key_p...  44.5 us
    ppermute x4, waiting for transfers between devices, passed_along(): lax.ppermute(array, axis, [(i, (i + by) % count) for i in range(count)])  42.7 us
    sub x4, matrix products, probabilities(): lifted = jnp.exp(scores - row_max)  30.8 us
    unnamed x133, local copies, waits for them, and re-layouts  27 us
    all_gather x2, waiting for transfers between devices, on_device(): every_half = lax.all_gather(my_half, 'ctx', axis=0, tiled=False)  26.7 us
    all_to_all x2, waiting for transfers between devices, on_device(): lax.all_to_all(jnp.stack(outgoing), 'ctx', split_axis=2, concat_axis=1, t...  13.9 us
    all_to_all x2, starting transfers between devices, on_device(): lax.all_to_all(jnp.stack(outgoing), 'ctx', split_axis=2, concat_axis=1, t...  13.7 us
  transfers between devices with their start and end apart: 15, of which 7 were waited for; matrix products, arithmetic and copies ran while one was open for 36% of the time, Pallas kernels for 0%

profile of v1, /device:TPU:1, one launch (start us, length us, event | category | flops | bytes accessed | tf_op | source)
XLA Modules:
  0.0 537.6 jit_solution(3037834608562657912)
XLA Ops:
  8.9 2.3 slice_convert_fusion.7
  19.6 8.4 %all-to-all-start.1 = ((bf16[3,32,16,512]{3,1,0,2:T(8,128)(2,1)}), bf16[3,32,16,512]{3,1,0,2:T(8,128)(2,1)}, u32[]{:S(2)}, u32[]{:S(2)}) async-start(bf16[3,32,16,512]{3,1,0,2:T(8,128)(2,1)} %pad_maximum_fusion.3), calls=%async_computation.1 | async-start | bytes 3145728 | tf_op jit(solution)/shard_map/all_to_all | solution.py:138
  37.1 13.9 %all-to-all-done.1 = bf16[3,32,16,512]{3,1,0,2:T(8,128)(2,1)} async-done(((bf16[3,32,16,512]{3,1,0,2:T(8,128)(2,1)}), bf16[3,32,16,512]{3,1,0,2:T(8,128)(2,1)}, u32[]{:S(2)}, u32[]{:S(2)}) %all-to-all-start.1) | async-done | bytes 1572896 | tf_op jit(solution)/shard_map/all_to_all | solution.py:138
  51.0 5.3 all-to-all-start
  56.5 3.0 fusion.231
  59.6 2.3 copy.318
  61.9 2.3 copy.324
  64.1 3.0 fusion.232
  67.2 2.3 copy.319
  69.4 2.3 copy.325
  71.7 2.3 fusion.233
  74.1 2.9 convert_bitcast_fusion.2
  78.3 2.4 pad_maximum_fusion
  80.7 8.5 %copy.303 = bf16[2,2,16,512,64]{4,3,1,0,2:T(8,128)(2,1)} copy(bf16[2,2,16,512,64]{3,4,2,0,1:T(8,128)(2,1)} %pad_maximum_fusion) | data formatting | bytes 8388608 | tf_op jit(solution)/shard_map/convert_element_type | solution.py:155
  89.2 13.8 %reshape.570 = bf16[4,16,32768]{2,0,1:T(4,128)(2,1)} reshape(bf16[2,2,16,512,64]{4,3,1,0,2:T(8,128)(2,1)} %copy.303) | data formatting | bytes 8388608 | tf_op jit(solution)/shard_map/convert_element_type | solution.py:155
  103.0 2.9 fusion.230
  108.8 2.3 pad_maximum_fusion.1
  111.1 8.5 %copy.309 = bf16[2,2,16,512,64]{4,3,1,0,2:T(8,128)(2,1)} copy(bf16[2,2,16,512,64]{3,4,2,0,1:T(8,128)(2,1)} %pad_maximum_fusion.1) | data formatting | bytes 8388608 | tf_op jit(solution)/shard_map/convert_element_type | solution.py:155
  119.6 13.8 %reshape.571 = bf16[4,16,32768]{2,0,1:T(4,128)(2,1)} reshape(bf16[2,2,16,512,64]{4,3,1,0,2:T(8,128)(2,1)} %copy.309) | data formatting | bytes 8388608 | tf_op jit(solution)/shard_map/convert_element_type | solution.py:155
  137.9 2.7 fusion.41
  140.6 1.9 reshape_reshape_squeeze.19
  142.6 2.0 reshape_reshape_squeeze.18
  144.5 1.9 reshape_reshape_squeeze.20
  146.5 2.2 copy.241
  148.6 2.0 reshape_reshape_squeeze.22
  150.6 2.0 reshape_reshape_squeeze.21
  152.6 2.0 reshape_reshape_squeeze.23
  154.6 2.1 copy.267
  156.7 2.0 reshape_squeeze.31
  158.7 2.2 fusion.235
  162.9 141.0 %all-reduce.5.cloned.1.call-done = (bf16[4,16,32768]{2,0,1:T(4,128)(2,1)}, bf16[4,16,32768]{2,0,1:T(4,128)(2,1)}) async-done(((bf16[4,16,32768]{2,0,1:T(4,128)(2,1)}, bf16[4,16,32768]{2,0,1:T(4,128)(2,1)}), (bf16[4,16,32768]{2,0,1:T(4,128)(2,1)}, bf16[4,16,32768]{2,0,1:T(4,128)(2,1)})) %all-reduce.5.cloned.1.call-update) | async-done | bytes 8388624
  306.8 2.6 collective-permute-start
  312.3 2.1 maximum_select_fusion.2
  315.1 7.7 %fusion.237 = (f32[4,512]{1,0:T(4,128)S(1)}, f32[4,512,1024]{1,2,0:T(8,128)}) fusion(pred[512,1024]{0,1:T(8,128)(4,1)} %get-tuple-element.60, bf16[512,4,128]{2,1,0:T(4,128)(2,1)} %reshape_reshape_squeeze.19, bf16[512,128]{1,0:T(8,128)(2,1)} %bitcast.544, bf16[512,128]{1,0:T(8,128)(2,1)S(1)} %get-tuple-element.41), kind=kOutput, calls=%fused_computation.277 | convolution fusion | flops 545784832 | bytes 9707520 | tf_op jit(solution)/shard_map/sub | solution.py:39
  322.9 4.8 fusion.28
  328.9 2.3 fusion.9
  336.9 7.7 %fusion.255 = (f32[4,512]{1,0:T(4,128)S(1)}, f32[4,512,1024]{1,2,0:T(8,128)}) fusion(pred[512,1024]{0,1:T(8,128)(4,1)} %get-tuple-element.58, bf16[512,4,128]{2,1,0:T(4,128)(2,1)} %reshape_reshape_squeeze.22, bf16[512,128]{1,0:T(8,128)(2,1)S(1)} %bitcast.541, bf16[512,128]{1,0:T(8,128)(2,1)} %get-tuple-element.49), kind=kOutput, calls=%fused_computation.279 | convolution fusion | flops 545784832 | bytes 9707520 | tf_op jit(solution)/shard_map/sub | solution.py:39
  344.6 4.8 fusion.29
  350.9 2.3 fusion.6
  353.3 1.9 copy-done.9
  356.9 7.7 %fusion.246 = (f32[4,512]{1,0:T(4,128)S(1)}, f32[4,512,1024]{1,2,0:T(8,128)}) fusion(pred[512,1024]{0,1:T(8,128)(4,1)} %get-tuple-element.57, bf16[512,4,128]{2,1,0:T(4,128)(2,1)} %reshape_reshape_squeeze.18, bf16[512,128]{1,0:T(8,128)(2,1)S(1)} %bitcast.545, bf16[512,128]{1,0:T(8,128)(2,1)} %get-tuple-element.42), kind=kOutput, calls=%fused_computation.278 | convolution fusion | flops 545784832 | bytes 9707520 | tf_op jit(solution)/shard_map/sub | solution.py:39
  366.3 5.1 fusion.58
  371.4 2.1 copy.238
  373.5 2.0 stack_reshape.4
  375.5 7.7 %fusion.264 = (f32[4,512]{1,0:T(4,128)S(1)}, f32[4,512,1024]{1,2,0:T(8,128)}) fusion(pred[512,1024]{0,1:T(8,128)(4,1)} %get-tuple-element.59, bf16[512,4,128]{2,1,0:T(4,128)(2,1)} %reshape_reshape_squeeze.21, bf16[512,128]{1,0:T(8,128)(2,1)S(1)} %bitcast.542, bf16[512,128]{1,0:T(8,128)(2,1)} %get-tuple-element.50), kind=kOutput, calls=%fused_computation.280 | convolution fusion | flops 545784832 | bytes 9707520 | tf_op jit(solution)/shard_map/sub | solution.py:39
  383.2 5.1 fusion.59
  388.3 2.2 copy.264
  390.5 2.1 stack_reshape.5
  392.5 4.0 fusion.50
  396.6 2.6 copy.246
  399.1 2.6 reshape.526
  401.8 4.0 fusion.55
  405.8 2.6 copy.272
  408.3 2.7 reshape.528
  411.0 1.8 fusion.228
  416.0 6.1 %all-to-all-start.2 = ((bf16[2,16,32,512]{3,2,0,1:T(8,128)(2,1)}), bf16[2,16,32,512]{3,2,0,1:T(8,128)(2,1)}, u32[]{:S(2)}, u32[]{:S(2)}) async-start(bf16[2,16,32,512]{3,2,0,1:T(8,128)(2,1)} %copy.253), calls=%async_computation.2 | async-start | bytes 2097152 | tf_op jit(solution)/shard_map/all_to_all | solution.py:209
  422.1 26.7 %all-gather.7.cloned.1.call-done = bf16[32,256,128]{2,1,0:T(8,128)(2,1)} async-done(((bf16[2,256,128]{2,1,0:T(8,128)(2,1)}), bf16[32,256,128]{2,1,0:T(8,128)(2,1)}) %all-gather.7.cloned.1.call-update) | async-done | bytes 2097168 | tf_op jit(solution)/shard_map/all_gather | solution.py:193
  448.8 1.8 fusion.229
  453.6 4.3 all-to-all-start.3
  463.7 11.6 %all-to-all-done.3 = bf16[2,16,32,512]{3,2,0,1:T(8,128)(2,1)} async-done(((bf16[2,16,32,512]{3,2,0,1:T(8,128)(2,1)}), bf16[2,16,32,512]{3,2,0,1:T(8,128)(2,1)}, u32[]{:S(2)}, u32[]{:S(2)}) %all-to-all-start.3) | async-done | bytes 1048608 | tf_op jit(solution)/shard_map/all_to_all | solution.py:209
  482.7 2.3 collective-permute-start.6
  485.7 27.7 %collective-permute-done.2 = bf16[32,8192]{1,0:T(8,128)(2,1)S(1)} collective-permute-done((bf16[32,8192]{1,0:T(8,128)(2,1)S(1)}, bf16[32,8192]{1,0:T(8,128)(2,1)S(1)}, u32[]{:S(2)}, u32[]{:S(2)}) %collective-permute-start.2) | collective-permute-done | bytes 524320 | tf_op jit(solution)/shard_map/ppermute | solution.py:11
  513.4 11.2 %collective-permute-done.5 = bf16[32,8192]{1,0:T(8,128)(2,1)S(1)} collective-permute-done((bf16[32,8192]{1,0:T(8,128)(2,1)S(1)}, bf16[32,8192]{1,0:T(8,128)(2,1)S(1)}, u32[]{:S(2)}, u32[]{:S(2)}) %collective-permute-start.5) | collective-permute-done | bytes 524320 | tf_op jit(solution)/shard_map/ppermute | solution.py:11
  525.8 3.7 collective-permute-done.7
  (217 shorter events, 67.6 us)
Async XLA Ops:
  7.2 4.0 copy-start
  7.2 5.8 %copy-start.49 = (f32[1,2,8192]{2,1,0:T(2,128)S(1)}, f32[1,2,8192]{2,1,0:T(2,128)}, u32[]{:S(2)}) copy-start(f32[1,2,8192]{2,1,0:T(2,128)} %param.14) | copy-start | bytes 196612
  7.2 7.1 %copy-start.2 = (bf16[1,2,32,8192]{3,2,1,0:T(8,128)(2,1)S(1)}, bf16[1,2,32,8192]{3,2,1,0:T(8,128)(2,1)}, u32[]{:S(2)}) copy-start(bf16[1,2,32,8192]{3,2,1,0:T(8,128)(2,1)} %param.11) | copy-start | bytes 3145732
  14.3 2.7 copy-start.41
  14.3 2.0 copy-start.7
  17.0 11.1 %copy-start.47 = (bf16[1,2,32,8,128]{4,3,2,1,0:T(8,128)(2,1)S(1)}, bf16[1,2,32,8,128]{4,3,2,1,0:T(8,128)(2,1)}, u32[]{:S(2)}) copy-start(bf16[1,2,32,8,128]{4,3,2,1,0:T(8,128)(2,1)} %param.12) | copy-start | bytes 393220
  18.3 11.0 %copy-start.48 = (bf16[1,2,32,8,128]{4,3,2,1,0:T(8,128)(2,1)S(1)}, bf16[1,2,32,8,128]{4,3,2,1,0:T(8,128)(2,1)}, u32[]{:S(2)}) copy-start(bf16[1,2,32,8,128]{4,3,2,1,0:T(8,128)(2,1)} %param.13) | copy-start | bytes 393220
  19.6 31.4 %all-to-all-start.1 = ((bf16[3,32,16,512]{3,1,0,2:T(8,128)(2,1)}), bf16[3,32,16,512]{3,1,0,2:T(8,128)(2,1)}, u32[]{:S(2)}, u32[]{:S(2)}) async-start(bf16[3,32,16,512]{3,1,0,2:T(8,128)(2,1)} %pad_maximum_fusion.3), calls=%async_computation.1 | async-start | bytes 3145728 | tf_op jit(solution)/shard_map/all_to_all | solution.py:138
  30.5 3.7 copy-start.29
  31.3 4.2 copy-start.43
  31.3 2.2 copy-start.4
  31.3 2.9 copy-start.30
  51.0 52.0 %all-to-all-start = ((bf16[4,32,16,512]{3,1,0,2:T(8,128)(2,1)}), bf16[4,32,16,512]{3,1,0,2:T(8,128)(2,1)}, u32[]{:S(2)}, u32[]{:S(2)}) async-start(bf16[4,32,16,512]{3,1,0,2:T(8,128)(2,1)} %pad_maximum_fusion.2), calls=%async_computation | async-start | bytes 4194304 | tf_op jit(solution)/shard_map/all_to_all | solution.py:138
  56.3 247.6 %all-reduce.5.cloned.1.call-start = ((), (), s32[]{:S(2)}) async-start(), calls=%async_computation.6 | async-start | bytes 16777216
  74.1 2.9 copy-start.20
  74.1 2.9 copy-start.21
  74.1 2.9 copy-start.14
  103.0 2.9 copy-start.26
  105.9 1.6 copy-start.12
  133.3 3.9 copy-start.51
  133.4 277.6 %all-gather.5.cloned.1.call-start = ((), (), s32[]{:S(2)}) async-start(), calls=%async_computation.4 | async-start | bytes 2228224 | tf_op jit(solution)/shard_map/all_gather | solution.py:193
  306.8 5.5 %collective-permute-start = (bf16[2,2,512,64]{3,2,1,0:T(8,128)(2,1)}, bf16[2,2,512,64]{3,2,1,0:T(8,128)(2,1)}, u32[]{:S(2)}, u32[]{:S(2)}) collective-permute-start(bf16[2,2,512,64]{3,2,1,0:T(8,128)(2,1)} %reshape.512), channel_id=1, source_target_pairs={{0,1},{1,0},{2,3},{3,2},{4,5},{5,4},{6,7},{7,6},{8,9},{9,8},{10,11... | collective-permute-start | bytes 786440 | tf_op jit(solution)/shard_map/ppermute | solution.py:16
  312.2 21.0 %collective-permute-start.3 = (bf16[2,2,512,64]{3,2,1,0:T(8,128)(2,1)}, bf16[2,2,512,64]{3,2,1,0:T(8,128)(2,1)}, u32[]{:S(2)}, u32[]{:S(2)}) collective-permute-start(bf16[2,2,512,64]{3,2,1,0:T(8,128)(2,1)} %reshape.515), channel_id=1, source_target_pairs={{0,1},{1,0},{2,3},{3,2},{4,5},{5,4},{6,7},{7,6},{8,9},{9,8},{10,11... | collective-permute-start | bytes 786440 | tf_op jit(solution)/shard_map/ppermute | solution.py:16
  315.1 7.7 %copy-start.38 = (bf16[512,128]{1,0:T(8,128)(2,1)}, bf16[512,128]{1,0:T(8,128)(2,1)S(1)}, u32[]{:S(2)}) copy-start(bf16[512,128]{1,0:T(8,128)(2,1)S(1)} %get-tuple-element.41) | copy-start | bytes 393220
  322.8 5.6 %slice-start.2 = ((s8[8388608]{0:T(1024)(128)(4,1)}), s8[4194304]{0:T(1024)(128)(4,1)S(1)}, s32[]{:S(2)}) async-start(s8[8388608]{0:T(1024)(128)(4,1)} %bitcast.491), calls=%async_computation.9 | async-start | bytes 8388608
  322.8 4.8 copy-start.18
  322.8 4.8 copy-start.33
  322.8 6.0 %slice-start.3 = ((s8[8388608]{0:T(1024)(128)(4,1)}), s8[4194304]{0:T(1024)(128)(4,1)S(1)}, s32[]{:S(2)}) async-start(s8[8388608]{0:T(1024)(128)(4,1)} %bitcast.491), calls=%async_computation.10 | async-start | bytes 8388608
  328.9 2.3 copy-start.35
  331.2 3.9 copy-start.8
  331.2 2.1 copy-start.19
  332.7 3.3 collective-permute-start.1
  336.6 112.1 %all-gather.7.cloned.1.call-start = ((), (), s32[]{:S(2)}) async-start(), calls=%async_computation.5 | async-start | bytes 2228224 | tf_op jit(solution)/shard_map/all_gather | solution.py:193
  344.5 6.3 %slice-start = ((s8[8388608]{0:T(1024)(128)(4,1)}), s8[4194304]{0:T(1024)(128)(4,1)S(1)}, s32[]{:S(2)}) async-start(s8[8388608]{0:T(1024)(128)(4,1)} %bitcast.489), calls=%async_computation.7 | async-start | bytes 8388608
  344.5 4.8 copy-start.17
  344.5 5.5 %copy-start.32 = (bf16[512,1,1,128]{3,0,2,1:T(8,128)(2,1)S(1)}, bf16[512,1,1,128]{3,0,2,1:T(8,128)(2,1)}, u32[]{:S(2)}) copy-start(bf16[512,1,1,128]{3,0,2,1:T(8,128)(2,1)} %copy.430) | copy-start | bytes 393220
  344.5 5.5 %copy-start.40 = (bf16[512,128]{1,0:T(8,128)(2,1)S(1)}, bf16[512,128]{1,0:T(8,128)(2,1)}, u32[]{:S(2)}) copy-start(bf16[512,128]{1,0:T(8,128)(2,1)} %get-tuple-element.48) | copy-start | bytes 393220
  344.6 6.3 %slice-start.1 = ((s8[8388608]{0:T(1024)(128)(4,1)}), s8[4194304]{0:T(1024)(128)(4,1)S(1)}, s32[]{:S(2)}) async-start(s8[8388608]{0:T(1024)(128)(4,1)} %bitcast.489), calls=%async_computation.8 | async-start | bytes 8388608
  350.1 5.8 %copy-start.36 = (bf16[1,512,128]{2,1,0:T(8,128)(2,1)}, bf16[1,512,128]{2,1,0:T(8,128)(2,1)S(1)}, u32[]{:S(2)}) copy-start(bf16[1,512,128]{2,1,0:T(8,128)(2,1)S(1)} %fusion.93) | copy-start | bytes 393220
  350.9 4.3 copy-start.34
  353.3 1.9 copy-start.9
  355.2 1.7 copy-start.31
  356.7 7.9 %collective-permute-start.4 = (bf16[2,512,128]{2,1,0:T(8,128)(2,1)}, bf16[2,512,128]{2,1,0:T(8,128)(2,1)}, u32[]{:S(2)}, u32[]{:S(2)}) collective-permute-start(bf16[2,512,128]{2,1,0:T(8,128)(2,1)} %pad_maximum_fusion.15), channel_id=1, source_target_pairs={{0,1},{1,0},{2,3},{3,2},{4,5},{5,4},{6,7},{7,6},{8,9},{9,8},{10,11... | collective-permute-start | bytes 786440 | tf_op jit(solution)/shard_map/ppermute | solution.py:16
  392.5 9.2 %copy-start.39 = (bf16[512,128]{1,0:T(8,128)(2,1)S(1)}, bf16[512,128]{1,0:T(8,128)(2,1)}, u32[]{:S(2)}) copy-start(bf16[512,128]{1,0:T(8,128)(2,1)} %get-tuple-element.49) | copy-start | bytes 393220
  411.0 1.9 copy-start.28
  411.0 2.6 copy-start.15
  412.9 1.5 copy-start.11
  416.0 37.6 %all-to-all-start.2 = ((bf16[2,16,32,512]{3,2,0,1:T(8,128)(2,1)}), bf16[2,16,32,512]{3,2,0,1:T(8,128)(2,1)}, u32[]{:S(2)}, u32[]{:S(2)}) async-start(bf16[2,16,32,512]{3,2,0,1:T(8,128)(2,1)} %copy.253), calls=%async_computation.2 | async-start | bytes 2097152 | tf_op jit(solution)/shard_map/all_to_all | solution.py:209
  448.8 1.9 copy-start.27
  448.8 2.6 copy-start.13
  450.6 1.5 copy-start.10
  453.6 21.7 %all-to-all-start.3 = ((bf16[2,16,32,512]{3,2,0,1:T(8,128)(2,1)}), bf16[2,16,32,512]{3,2,0,1:T(8,128)(2,1)}, u32[]{:S(2)}, u32[]{:S(2)}) async-start(bf16[2,16,32,512]{3,2,0,1:T(8,128)(2,1)} %copy.279), calls=%async_computation.3 | async-start | bytes 2097152 | tf_op jit(solution)/shard_map/all_to_all | solution.py:209
  459.7 3.5 copy-start.42
  461.6 15.8 %copy-start.44 = (f32[16,512]{1,0:T(8,128)S(1)}, f32[16,512]{1,0:T(8,128)}, u32[]{:S(2)}) copy-start(f32[16,512]{1,0:T(8,128)} %copy-done.43) | copy-start | bytes 98308
  477.1 2.1 copy-start.1
  477.2 2.1 copy-start.16
  478.0 4.0 copy-start.3
  478.0 4.0 copy-start.5
  478.0 4.0 copy-start.45
  478.0 4.0 copy-start.46
  479.5 33.9 %collective-permute-start.2 = (bf16[32,8192]{1,0:T(8,128)(2,1)S(1)}, bf16[32,8192]{1,0:T(8,128)(2,1)S(1)}, u32[]{:S(2)}, u32[]{:S(2)}) collective-permute-start(bf16[32,8192]{1,0:T(8,128)(2,1)S(1)} %get-tuple-element.31), channel_id=1, source_target_pairs={{0,16},{16,32},{32,48},{48,64},{64,80},{80,96},{96,112},{112,128},... | collective-permute-start | bytes 1572872 | tf_op jit(solution)/shard_map/ppermute | solution.py:11
  480.7 44.0 %collective-permute-start.5 = (bf16[32,8192]{1,0:T(8,128)(2,1)S(1)}, bf16[32,8192]{1,0:T(8,128)(2,1)S(1)}, u32[]{:S(2)}, u32[]{:S(2)}) collective-permute-start(bf16[32,8192]{1,0:T(8,128)(2,1)S(1)} %get-tuple-element.32), channel_id=1, source_target_pairs={{0,16},{16,32},{32,48},{48,64},{64,80},{80,96},{96,112},{112,128},... | collective-permute-start | bytes 1572872 | tf_op jit(solution)/shard_map/ppermute | solution.py:11
  482.7 43.1 %collective-permute-start.6 = (bf16[32,8192]{1,0:T(8,128)(2,1)S(1)}, bf16[32,8192]{1,0:T(8,128)(2,1)S(1)}, u32[]{:S(2)}, u32[]{:S(2)}) collective-permute-start(bf16[32,8192]{1,0:T(8,128)(2,1)S(1)} %get-tuple-element.10), channel_id=1, source_target_pairs={{0,240},{16,0},{32,16},{48,32},{64,48},{80,64},{96,80},{112,96},{1... | collective-permute-start | bytes 1572872 | tf_op jit(solution)/shard_map/ppermute | solution.py:11
  485.0 44.5 %collective-permute-start.7 = (bf16[32,8192]{1,0:T(8,128)(2,1)S(1)}, bf16[32,8192]{1,0:T(8,128)(2,1)S(1)}, u32[]{:S(2)}, u32[]{:S(2)}) collective-permute-start(bf16[32,8192]{1,0:T(8,128)(2,1)S(1)} %get-tuple-element.11), channel_id=1, source_target_pairs={{0,240},{16,0},{32,16},{48,32},{64,48},{80,64},{96,80},{112,96},{1... | collective-permute-start | bytes 1572872 | tf_op jit(solution)/shard_map/ppermute | solution.py:11
  (7 other events, 7.9 us)
Sparse Core Ops, SparseCore 0:
  133.5 170.3 all-reduce.4
  336.8 52.9 all-gather.4
  392.5 56.1 all-gather.6
